TPU v7x, 256 devices: a whole 4x4x8 slice. The times are simulated.
256 devices in a mesh: expert: 128 (over z, x, y), dp: 2 (over core).
Axes of the slice: x: 4, y: 4, z: 8, core: 2. Of those that a mesh axis runs over, the one named last changes fastest.
Arguments:
- hidden: bfloat16 [32768, 8, 1024], P(('expert', 'dp')), may hold values from -8 to 8
- routes: int32 [32768, 8], P(('expert', 'dp')), may hold values from 0 to 127, as said below
- slots: int32 [32768, 8], P(('expert', 'dp')), may hold values from 0 to 15, as said below
- down_weight: bfloat16 [128, 1024, 7168], P('expert', None, 'dp'), may hold values from -0.1875 to 0.1875
- omega: bfloat16 [128, 1024, 256], P('expert'), may hold values from -0.1875 to 0.1875
Outputs:
- whitening: float32 [128, 1024, 1024], P('expert', 'dp')
- basis: float32 [2, 3584, 256], P('dp', 'expert')
Inputs may be any that keep to these rules, and one draw needn't show every extreme that they name: `routes`: each token names 8 different experts. Among the tokens of one device no expert is named more than 16 times, and one expert is named exactly 16 times by the tokens of every device. Among the tokens of one device, the pairs that name one expert have different slots.
All inputs are finite; a program needn't handle non-finite values.
Results may differ from a plain program's by a relative error of at most 0.0032.
Values may be sent and summed in bfloat16 or wider, within the bound.
No kernel may reach another device: no remote copies, remote signals or barrier semaphores. Data moves between devices by JAX's collectives and lax.ppermute only.
A program may use at most 128 MiB of HBM per device.

v0:
```python
import math
import jax
import jax.numpy as jnp
from jax import lax
from jax.sharding import PartitionSpec as P

damping = 0.1
jitter = 1e-06


def contract(left, right):
    return lax.dot_general(
        left, right, (((0,), (0,)), ((), ())), preferred_element_type=jnp.float32
    )


def local(hidden, routes, slots, down_weight, omega):
    n_exp = lax.axis_size("expert")
    n_dp = lax.axis_size("dp")
    tok_rows, n_route, hid_width = hidden.shape
    capacity = 2 * tok_rows * n_route // n_exp
    n_slot = n_exp * n_dp * capacity
    slot_index = (routes * capacity + slots).reshape(-1)
    outgoing = jnp.zeros((n_exp * capacity, hid_width), jnp.bfloat16)
    outgoing = (
        outgoing.at[slot_index]
        .set(hidden.reshape(-1, hid_width))
        .reshape(n_exp, capacity, hid_width)
    )
    received = lax.all_to_all(outgoing, "expert", split_axis=0, concat_axis=0, tiled=True).reshape(
        n_exp * capacity, hid_width
    )
    gram_mat = lax.psum(contract(received, received), "dp") / n_slot
    identity_mat = jnp.eye(hid_width, dtype=jnp.float32)
    damped = gram_mat + (damping * jnp.mean(jnp.diagonal(gram_mat)) + jitter) * identity_mat
    whitening = jnp.linalg.cholesky(damped)
    test_mat = jnp.dot(
        whitening, omega[0].astype(jnp.float32), precision=lax.Precision.HIGHEST
    ).astype(jnp.bfloat16)
    down_half = down_weight[0]
    half_cols = down_half.shape[1]
    row_share = half_cols // n_exp
    whole_half = lax.psum(contract(down_half, test_mat), "expert")
    small_gram = lax.psum(jnp.dot(whole_half.T, whole_half, precision=lax.Precision.HIGHEST), "dp")
    sketch = lax.dynamic_slice_in_dim(
        whole_half, lax.axis_index("expert") * row_share, row_share, 0
    )
    qr_factor = jnp.linalg.cholesky(small_gram)
    basis_rows = jax.scipy.linalg.solve_triangular(qr_factor, sketch.T, lower=True).T * math.sqrt(
        half_cols * n_dp
    )
    own_rows = lax.dynamic_slice_in_dim(
        whitening, lax.axis_index("dp") * (hid_width // n_dp), hid_width // n_dp, 0
    )
    return (own_rows[None], basis_rows[None])


def solution(mesh):
    placed = (
        P(("expert", "dp"), None, None),
        P(("expert", "dp"), None),
        P(("expert", "dp"), None),
        P("expert", None, "dp"),
        P("expert", None, None),
    )
    return jax.shard_map(
        local,
        mesh=mesh,
        in_specs=placed,
        out_specs=(P("expert", "dp", None), P("dp", "expert", None)),
        check_vma=False,
    )
```

profile of v0, /device:TPU:1, one launch (start us, length us, event | category | flops | bytes accessed | tf_op | source)
XLA Modules:
  0.0 775.2 jit_solution(16030494886946830001)
XLA Ops:
  16.7 110.1 %all_to_all.5 = bf16[128,16,1024]{2,1,0:T(8,128)(2,1)S(1)} all-to-all(bf16[128,16,1024]{2,1,0:T(8,128)(2,1)} %bitcast.109), channel_id=1, replica_groups=mesh['expert'=128,'dp'=2] {'expert'}, dimensions={0} | all-to-all | bytes 8388608 | tf_op jit(solution)/shard_map/all_to_all | solution.py:30
  133.0 38.1 %all-reduce.6.cloned.1.call-done = f32[1024,1024]{0,1:T(8,128)} async-done(((f32[1024,1024]{0,1:T(8,128)}), f32[1024,1024]{0,1:T(8,128)}) %all-reduce.6.cloned.1.call-update) | async-done | bytes 4194320 | tf_op jit(solution)/shard_map/psum | solution.py:33
  176.2 16.8 %gather_fusion = f32[1024]{0:T(1024)S(1)} fusion(f32[1024,1024]{0,1:T(8,128)} %broadcast_multiply_fusion, s32[1024]{0:T(1024)S(1)} %bitcast.108), kind=kCustom, calls=%fused_computation | custom fusion | bytes 16384 | tf_op jit(solution)/shard_map/jit(diagonal)/cond/branch_0_fun/gather | solution.py:35
  211.2 11.7 %cholesky.249 = f32[128,128]{1,0:T(8,128)S(1)} custom-call(f32[128,128]{1,0:T(8,128)S(1)} %cholesky.650), custom_call_target="Cholesky" | custom-call | tf_op jit(solution)/shard_map/jit(cholesky)/cholesky | solution.py:36
  223.0 9.8 %custom-call.67 = f32[1,128,128]{1,2,0:T(8,128)S(1)} custom-call(f32[1,128,128]{2,1,0:T(8,128)S(1)} %get-tuple-element.44), custom_call_target="InvertDiagBlocksLowerTriangular" | custom-call | tf_op jit(solution)/shard_map/jit(cholesky)/cholesky | solution.py:36
  236.2 11.7 %cholesky.274 = f32[128,128]{1,0:T(8,128)S(1)} custom-call(f32[128,128]{1,0:T(8,128)S(1)} %cholesky.654), custom_call_target="Cholesky" | custom-call | tf_op jit(solution)/shard_map/jit(cholesky)/cholesky | solution.py:36
  250.7 9.8 %custom-call.68 = f32[1,128,128]{1,2,0:T(8,128)S(1)} custom-call(f32[1,128,128]{2,1,0:T(8,128)S(1)} %get-tuple-element.42), custom_call_target="InvertDiagBlocksLowerTriangular" | custom-call | tf_op jit(solution)/shard_map/jit(cholesky)/cholesky | solution.py:36
  266.0 11.7 %cholesky.299 = f32[128,128]{1,0:T(8,128)S(1)} custom-call(f32[128,128]{1,0:T(8,128)S(1)} %cholesky.659), custom_call_target="Cholesky" | custom-call | tf_op jit(solution)/shard_map/jit(cholesky)/cholesky | solution.py:36
  278.5 9.8 %custom-call.69 = f32[1,128,128]{1,2,0:T(8,128)S(1)} custom-call(f32[1,128,128]{2,1,0:T(8,128)S(1)} %get-tuple-element.40), custom_call_target="InvertDiagBlocksLowerTriangular" | custom-call | tf_op jit(solution)/shard_map/jit(cholesky)/cholesky | solution.py:36
  293.1 11.7 %cholesky.539 = f32[128,128]{1,0:T(8,128)S(1)} custom-call(f32[128,128]{1,0:T(8,128)S(1)} %cholesky.664), custom_call_target="Cholesky" | custom-call | tf_op jit(solution)/shard_map/jit(cholesky)/cholesky | solution.py:36
  305.6 9.8 %custom-call.70 = f32[1,128,128]{1,2,0:T(8,128)S(1)} custom-call(f32[1,128,128]{2,1,0:T(8,128)S(1)} %get-tuple-element.38), custom_call_target="InvertDiagBlocksLowerTriangular" | custom-call | tf_op jit(solution)/shard_map/jit(cholesky)/cholesky | solution.py:36
  319.7 11.8 %cholesky.558 = f32[128,128]{1,0:T(8,128)S(1)} custom-call(f32[128,128]{1,0:T(8,128)S(1)} %cholesky.669), custom_call_target="Cholesky" | custom-call | tf_op jit(solution)/shard_map/jit(cholesky)/cholesky | solution.py:36
  332.3 9.8 %custom-call.71 = f32[1,128,128]{1,2,0:T(8,128)S(1)} custom-call(f32[1,128,128]{2,1,0:T(8,128)S(1)} %get-tuple-element.36), custom_call_target="InvertDiagBlocksLowerTriangular" | custom-call | tf_op jit(solution)/shard_map/jit(cholesky)/cholesky | solution.py:36
  346.4 11.7 %cholesky.578 = f32[128,128]{1,0:T(8,128)S(1)} custom-call(f32[128,128]{1,0:T(8,128)S(1)} %cholesky.674), custom_call_target="Cholesky" | custom-call | tf_op jit(solution)/shard_map/jit(cholesky)/cholesky | solution.py:36
  358.8 9.8 %custom-call.72 = f32[1,128,128]{1,2,0:T(8,128)S(1)} custom-call(f32[1,128,128]{2,1,0:T(8,128)S(1)} %get-tuple-element.34), custom_call_target="InvertDiagBlocksLowerTriangular" | custom-call | tf_op jit(solution)/shard_map/jit(cholesky)/cholesky | solution.py:36
  372.5 11.7 %cholesky.598 = f32[128,128]{1,0:T(8,128)S(1)} custom-call(f32[128,128]{1,0:T(8,128)S(1)} %cholesky.679), custom_call_target="Cholesky" | custom-call | tf_op jit(solution)/shard_map/jit(cholesky)/cholesky | solution.py:36
  385.0 9.8 %custom-call.77 = f32[1,128,128]{1,2,0:T(8,128)S(1)} custom-call(f32[1,128,128]{2,1,0:T(8,128)S(1)} %get-tuple-element.32), custom_call_target="InvertDiagBlocksLowerTriangular" | custom-call | tf_op jit(solution)/shard_map/jit(cholesky)/cholesky/custom-call.17 | solution.py:36
  397.9 11.7 %cholesky.612 = f32[128,128]{1,0:T(8,128)S(1)} custom-call(f32[128,128]{1,0:T(8,128)S(1)} %convolution_subtract_fusion.8), custom_call_target="Cholesky" | custom-call | tf_op jit(solution)/shard_map/jit(cholesky)/cholesky | solution.py:36
  435.8 229.8 %all-reduce.8.cloned.1.call-done = f32[3584,256]{0,1:T(8,128)} async-done(((f32[3584,256]{0,1:T(8,128)}), f32[3584,256]{0,1:T(8,128)}) %all-reduce.8.cloned.1.call-update) | async-done | bytes 3670032 | tf_op jit(solution)/shard_map/psum | solution.py:43
  680.0 24.5 %all-reduce.10.cloned.1.call-done = f32[256,256]{0,1:T(8,128)} async-done(((f32[256,256]{0,1:T(8,128)}), f32[256,256]{0,1:T(8,128)}) %all-reduce.10.cloned.1.call-update) | async-done | bytes 262160 | tf_op jit(solution)/shard_map/psum | solution.py:44
  706.6 11.7 %cholesky.625 = f32[128,128]{1,0:T(8,128)S(1)} custom-call(f32[128,128]{1,0:T(8,128)S(1)} %cholesky.683), custom_call_target="Cholesky" | custom-call | tf_op jit(solution)/shard_map/jit(cholesky)/cholesky | solution.py:48
  718.4 9.8 %custom-call.78 = f32[1,128,128]{1,2,0:T(8,128)S(1)} custom-call(f32[1,128,128]{2,1,0:T(8,128)S(1)} %get-tuple-element.30), custom_call_target="InvertDiagBlocksLowerTriangular" | custom-call | tf_op jit(solution)/shard_map/jit(cholesky)/cholesky/custom-call.17 | solution.py:48
  728.7 11.7 %cholesky.634 = f32[128,128]{1,0:T(8,128)S(1)} custom-call(f32[128,128]{1,0:T(8,128)S(1)} %convolution_subtract_fusion.7), custom_call_target="Cholesky" | custom-call | tf_op jit(solution)/shard_map/jit(cholesky)/cholesky | solution.py:48
  747.2 19.9 %custom-call.73 = f32[2,128,128]{1,2,0:T(8,128)S(1)} custom-call(f32[2,128,128]{2,1,0:T(8,128)S(1)} %get-tuple-element.10), custom_call_target="InvertDiagBlocksLowerTriangular" | custom-call | tf_op jit(solution)/shard_map/jit(_solve_triangular)/triangular_solve | solution.py:49
  (115 shorter events, 122.9 us)
Async XLA Ops:
  7.2 1.6 copy-start
  7.2 164.0 %all-reduce.6.cloned.1.call-start = ((), (), s32[]{:S(2)}) async-start(), calls=%async_computation.1 | async-start | bytes 8388608 | tf_op jit(solution)/shard_map/psum | solution.py:33
  133.0 532.6 %all-reduce.8.cloned.1.call-start = ((), (), s32[]{:S(2)}) async-start(), calls=%async_computation.2 | async-start | bytes 7340032 | tf_op jit(solution)/shard_map/psum | solution.py:43
  209.3 1.9 copy-start.3
  420.0 4.7 copy-start.4
  422.8 1.9 copy-start.2
  435.7 268.8 %all-reduce.10.cloned.1.call-start = ((), (), s32[]{:S(2)}) async-start(), calls=%async_computation.3 | async-start | bytes 524288 | tf_op jit(solution)/shard_map/psum | solution.py:44
  672.6 95.9 %copy-start.1 = (bf16[128,8,1024]{2,1,0:T(8,128)(2,1)S(1)}, bf16[128,8,1024]{2,1,0:T(8,128)(2,1)}, u32[]{:S(2)}) copy-start(bf16[128,8,1024]{2,1,0:T(8,128)(2,1)} %param.7) | copy-start | bytes 6291460
Sparse Core Ops, SparseCore 0:
  133.1 38.0 all-reduce.5
  435.8 229.7 all-reduce.7
  672.7 31.7 all-reduce.9
where the time goes:
time: 784 us; the launch traced here: 775 us
  waiting for transfers between devices  293 us (37%)
  other arithmetic  242 us (31%)
  blocking collectives  110 us (14%)
  local copies, waits for them, and re-layouts  57 us (7%)
  matrix products  52.5 us (7%)
  between operations  21.4 us (3%)
    psum x1, waiting for transfers between devices, local(): whole_half = lax.psum(contract(down_half, test_mat), 'expert')  230 us
    another operation x30, other arithmetic, local(): whitening = jnp.linalg.cholesky(damped)  167 us
    all_to_all x1, blocking collectives, local(): lax.all_to_all(outgoing, 'expert', split_axis=0, concat_axis=0, tiled=True)  110 us
    psum x1, waiting for transfers between devices, local(): gram_mat = lax.psum(contract(received, received), 'dp') / n_slot  38.1 us
    another operation x7, other arithmetic, local(): qr_factor = jnp.linalg.cholesky(small_gram)  34.6 us
    another operation x14, matrix products, local(): whitening = jnp.linalg.cholesky(damped)  27.2 us
    psum x1, waiting for transfers between devices, local(): lax.psum(jnp.dot(whole_half.T, whole_half, precision=lax.Precision.HIGHES...  24.5 us
    another operation x3, other arithmetic, local(): jax.scipy.linalg.solve_triangular(qr_factor, sketch.T, lower=True)  19.9 us
  transfers between devices with their start and end apart: 3, of which 3 were waited for; matrix products, arithmetic and copies ran while one was open for 1% of the time, Pallas kernels for 0%

commit v1 on v0

--- a/solution.py
+++ b/solution.py
@@ -41,7 +41,10 @@
     half_cols = down_half.shape[1]
     row_share = half_cols // n_exp
     whole_half = lax.psum(contract(down_half, test_mat), "expert")
-    small_gram = lax.psum(jnp.dot(whole_half.T, whole_half, precision=lax.Precision.HIGHEST), "dp")
+    small_gram = jnp.sum(
+        lax.all_gather(jnp.dot(whole_half.T, whole_half, precision=lax.Precision.HIGHEST), "dp"),
+        axis=0,
+    )
     sketch = lax.dynamic_slice_in_dim(
         whole_half, lax.axis_index("expert") * row_share, row_share, 0
     )

time: 784 us -> 758 us (0.967)
  waiting for transfers between devices: 293 us -> 264 us
    psum x1 -> x0, waiting for transfers between devices: 24.5 us -> none  [local(): lax.psum(jnp.dot(whole_half.T, whole_half, precision=lax.Precision.HIGHES...]
  transfers between devices with their start and end apart: 3 -> 2, of which waited for: 3 -> 2; matrix products, arithmetic and copies ran while one was open for 1% -> 0% of each run, Pallas kernels for 0% -> 0%
where the time goes in v1:
time: 758 us; the launch traced here: 749 us
  waiting for transfers between devices  264 us (35%)
  other arithmetic  241 us (32%)
  blocking collectives  117 us (15%)
  local copies, waits for them, and re-layouts  53.3 us (7%)
  matrix products  51.9 us (7%)
  between operations  21.7 us (3%)
    psum x1, waiting for transfers between devices, local(): whole_half = lax.psum(contract(down_half, test_mat), 'expert')  226 us
    another operation x30, other arithmetic, local(): whitening = jnp.linalg.cholesky(damped)  167 us
    all_to_all x1, blocking collectives, local(): lax.all_to_all(outgoing, 'expert', split_axis=0, concat_axis=0, tiled=True)  110 us
    psum x1, waiting for transfers between devices, local(): gram_mat = lax.psum(contract(received, received), 'dp') / n_slot  38.1 us
    another operation x7, other arithmetic, local(): qr_factor = jnp.linalg.cholesky(small_gram)  34.7 us
    another operation x14, matrix products, local(): whitening = jnp.linalg.cholesky(damped)  27.2 us
    another operation x3, other arithmetic, local(): jax.scipy.linalg.solve_triangular(qr_factor, sketch.T, lower=True)  19.7 us
    gather x1, local copies, waits for them, and re-layouts, local(): jnp.diagonal(gram_mat)  16.8 us
  transfers between devices with their start and end apart: 2, of which 2 were waited for; matrix products, arithmetic and copies ran while one was open for 0% of the time, Pallas kernels for 0%

profile of v1, /device:TPU:1, one launch (start us, length us, event | category | flops | bytes accessed | tf_op | source)
XLA Modules:
  0.0 749.3 jit_solution(12923769956063512872)
XLA Ops:
  8.8 7.9 %scatter_custom_fusion = bf16[2048,1024]{1,0:T(8,128)(2,1)} fusion(s32[1024]{0:T(1024)S(1)} %bitcast.113, bf16[128,8,1024]{2,1,0:T(8,128)(2,1)S(1)} %copy-done, bf16[]{:T(256)} %constant.347.clone.1), kind=kCustom, calls=%fused_computation.14 | custom fusion | bytes 6291458 | tf_op jit(solution)/shard_map/scatter | solution.py:27
  16.7 110.1 %all_to_all.5 = bf16[128,16,1024]{2,1,0:T(8,128)(2,1)S(1)} all-to-all(bf16[128,16,1024]{2,1,0:T(8,128)(2,1)} %bitcast.110), channel_id=1, replica_groups=mesh['expert'=128,'dp'=2] {'expert'}, dimensions={0} | all-to-all | bytes 8388608 | tf_op jit(solution)/shard_map/all_to_all | solution.py:30
  133.0 38.1 %all-reduce.5.cloned.1.call-done = f32[1024,1024]{0,1:T(8,128)} async-done(((f32[1024,1024]{0,1:T(8,128)}), f32[1024,1024]{0,1:T(8,128)}) %all-reduce.5.cloned.1.call-update) | async-done | bytes 4194320 | tf_op jit(solution)/shard_map/psum | solution.py:33
  176.2 16.8 %gather_fusion = f32[1024]{0:T(1024)S(1)} fusion(f32[1024,1024]{0,1:T(8,128)} %broadcast_multiply_fusion, s32[1024]{0:T(1024)S(1)} %bitcast.109), kind=kCustom, calls=%fused_computation | custom fusion | bytes 16384 | tf_op jit(solution)/shard_map/jit(diagonal)/cond/branch_0_fun/gather | solution.py:35
  211.2 11.7 %cholesky.249 = f32[128,128]{1,0:T(8,128)S(1)} custom-call(f32[128,128]{1,0:T(8,128)S(1)} %cholesky.650), custom_call_target="Cholesky" | custom-call | tf_op jit(solution)/shard_map/jit(cholesky)/cholesky | solution.py:36
  223.0 9.8 %custom-call.67 = f32[1,128,128]{1,2,0:T(8,128)S(1)} custom-call(f32[1,128,128]{2,1,0:T(8,128)S(1)} %get-tuple-element.44), custom_call_target="InvertDiagBlocksLowerTriangular" | custom-call | tf_op jit(solution)/shard_map/jit(cholesky)/cholesky | solution.py:36
  236.2 11.7 %cholesky.274 = f32[128,128]{1,0:T(8,128)S(1)} custom-call(f32[128,128]{1,0:T(8,128)S(1)} %cholesky.654), custom_call_target="Cholesky" | custom-call | tf_op jit(solution)/shard_map/jit(cholesky)/cholesky | solution.py:36
  250.7 9.8 %custom-call.68 = f32[1,128,128]{1,2,0:T(8,128)S(1)} custom-call(f32[1,128,128]{2,1,0:T(8,128)S(1)} %get-tuple-element.42), custom_call_target="InvertDiagBlocksLowerTriangular" | custom-call | tf_op jit(solution)/shard_map/jit(cholesky)/cholesky | solution.py:36
  266.0 11.7 %cholesky.299 = f32[128,128]{1,0:T(8,128)S(1)} custom-call(f32[128,128]{1,0:T(8,128)S(1)} %cholesky.659), custom_call_target="Cholesky" | custom-call | tf_op jit(solution)/shard_map/jit(cholesky)/cholesky | solution.py:36
  278.5 9.8 %custom-call.69 = f32[1,128,128]{1,2,0:T(8,128)S(1)} custom-call(f32[1,128,128]{2,1,0:T(8,128)S(1)} %get-tuple-element.40), custom_call_target="InvertDiagBlocksLowerTriangular" | custom-call | tf_op jit(solution)/shard_map/jit(cholesky)/cholesky | solution.py:36
  293.1 11.7 %cholesky.539 = f32[128,128]{1,0:T(8,128)S(1)} custom-call(f32[128,128]{1,0:T(8,128)S(1)} %cholesky.664), custom_call_target="Cholesky" | custom-call | tf_op jit(solution)/shard_map/jit(cholesky)/cholesky | solution.py:36
  305.6 9.8 %custom-call.70 = f32[1,128,128]{1,2,0:T(8,128)S(1)} custom-call(f32[1,128,128]{2,1,0:T(8,128)S(1)} %get-tuple-element.38), custom_call_target="InvertDiagBlocksLowerTriangular" | custom-call | tf_op jit(solution)/shard_map/jit(cholesky)/cholesky | solution.py:36
  319.7 11.8 %cholesky.558 = f32[128,128]{1,0:T(8,128)S(1)} custom-call(f32[128,128]{1,0:T(8,128)S(1)} %cholesky.669), custom_call_target="Cholesky" | custom-call | tf_op jit(solution)/shard_map/jit(cholesky)/cholesky | solution.py:36
  332.3 9.8 %custom-call.71 = f32[1,128,128]{1,2,0:T(8,128)S(1)} custom-call(f32[1,128,128]{2,1,0:T(8,128)S(1)} %get-tuple-element.36), custom_call_target="InvertDiagBlocksLowerTriangular" | custom-call | tf_op jit(solution)/shard_map/jit(cholesky)/cholesky | solution.py:36
  346.4 11.7 %cholesky.578 = f32[128,128]{1,0:T(8,128)S(1)} custom-call(f32[128,128]{1,0:T(8,128)S(1)} %cholesky.674), custom_call_target="Cholesky" | custom-call | tf_op jit(solution)/shard_map/jit(cholesky)/cholesky | solution.py:36
  358.8 9.8 %custom-call.72 = f32[1,128,128]{1,2,0:T(8,128)S(1)} custom-call(f32[1,128,128]{2,1,0:T(8,128)S(1)} %get-tuple-element.34), custom_call_target="InvertDiagBlocksLowerTriangular" | custom-call | tf_op jit(solution)/shard_map/jit(cholesky)/cholesky | solution.py:36
  372.5 11.7 %cholesky.598 = f32[128,128]{1,0:T(8,128)S(1)} custom-call(f32[128,128]{1,0:T(8,128)S(1)} %cholesky.679), custom_call_target="Cholesky" | custom-call | tf_op jit(solution)/shard_map/jit(cholesky)/cholesky | solution.py:36
  385.0 9.8 %custom-call.77 = f32[1,128,128]{1,2,0:T(8,128)S(1)} custom-call(f32[1,128,128]{2,1,0:T(8,128)S(1)} %get-tuple-element.32), custom_call_target="InvertDiagBlocksLowerTriangular" | custom-call | tf_op jit(solution)/shard_map/jit(cholesky)/cholesky/custom-call.17 | solution.py:36
  397.9 11.7 %cholesky.612 = f32[128,128]{1,0:T(8,128)S(1)} custom-call(f32[128,128]{1,0:T(8,128)S(1)} %convolution_subtract_fusion.8), custom_call_target="Cholesky" | custom-call | tf_op jit(solution)/shard_map/jit(cholesky)/cholesky | solution.py:36
  439.3 226.3 %all-reduce.7.cloned.1.call-done = f32[3584,256]{0,1:T(8,128)} async-done(((f32[3584,256]{0,1:T(8,128)}), f32[3584,256]{0,1:T(8,128)}) %all-reduce.7.cloned.1.call-update) | async-done | bytes 3670032 | tf_op jit(solution)/shard_map/psum | solution.py:43
  679.2 11.7 %cholesky.625 = f32[128,128]{1,0:T(8,128)S(1)} custom-call(f32[128,128]{1,0:T(8,128)S(1)} %cholesky.683), custom_call_target="Cholesky" | custom-call | tf_op jit(solution)/shard_map/jit(cholesky)/cholesky | solution.py:51
  691.0 9.8 %custom-call.78 = f32[1,128,128]{1,2,0:T(8,128)S(1)} custom-call(f32[1,128,128]{2,1,0:T(8,128)S(1)} %get-tuple-element.30), custom_call_target="InvertDiagBlocksLowerTriangular" | custom-call | tf_op jit(solution)/shard_map/jit(cholesky)/cholesky/custom-call.17 | solution.py:51
  701.3 11.7 %cholesky.634 = f32[128,128]{1,0:T(8,128)S(1)} custom-call(f32[128,128]{1,0:T(8,128)S(1)} %convolution_subtract_fusion.7), custom_call_target="Cholesky" | custom-call | tf_op jit(solution)/shard_map/jit(cholesky)/cholesky | solution.py:51
  720.0 19.7 %custom-call.73 = f32[2,128,128]{1,2,0:T(8,128)S(1)} custom-call(f32[2,128,128]{2,1,0:T(8,128)S(1)} %get-tuple-element.10), custom_call_target="InvertDiagBlocksLowerTriangular" | custom-call | tf_op jit(solution)/shard_map/jit(_solve_triangular)/triangular_solve | solution.py:52
  (114 shorter events, 117.0 us)
Async XLA Ops:
  7.2 1.6 copy-start
  7.2 164.0 %all-reduce.5.cloned.1.call-start = ((), (), s32[]{:S(2)}) async-start(), calls=%async_computation.1 | async-start | bytes 8388608 | tf_op jit(solution)/shard_map/psum | solution.py:33
  133.0 532.6 %all-reduce.7.cloned.1.call-start = ((), (), s32[]{:S(2)}) async-start(), calls=%async_computation.2 | async-start | bytes 7340032 | tf_op jit(solution)/shard_map/psum | solution.py:43
  209.3 1.9 copy-start.3
  420.0 4.7 copy-start.4
  422.8 1.9 copy-start.2
  665.6 76.6 %copy-start.1 = (bf16[128,8,1024]{2,1,0:T(8,128)(2,1)S(1)}, bf16[128,8,1024]{2,1,0:T(8,128)(2,1)}, u32[]{:S(2)}) copy-start(bf16[128,8,1024]{2,1,0:T(8,128)(2,1)} %param.7) | copy-start | bytes 6291460
Sparse Core Ops, SparseCore 0:
  133.1 38.0 all-reduce.4
  435.8 229.7 all-reduce.6
